TPU v7x, 32 devices: a whole 2x2x4 slice. The times are simulated.
32 devices in a mesh: shard: 4 (over z), rep: 8 (over y, x, core).
Axes of the slice: x: 2, y: 2, z: 4, core: 2. Of those that a mesh axis runs over, the one named last changes fastest.
Arguments:
- grads: bfloat16 [1, 8192, 28672], P(None, 'shard', 'rep'), may hold values from -81 to 81
- seeds: int32 [1], replicated, may hold values from 0 to 999999
Outputs:
- projected: bfloat16 [512, 1, 28672], P('shard', None, 'rep')
All inputs are finite; a program needn't handle non-finite values.
Results may differ from a plain program's by a relative error of at most 0.0056.
Values may be sent and summed in bfloat16 or wider, within the bound.
No kernel may reach another device: no remote copies, remote signals or barrier semaphores. Data moves between devices by JAX's collectives and lax.ppermute only.
A program may use at most 128 MiB of HBM per device.

v0:
```python
import jax
import jax.numpy as jnp
from jax import lax
from jax.sharding import PartitionSpec as P

RANK = 512
mix_first = 668265263
mix_second = -2048144789
mix_third = -1028477387


def sketch_table(seeds, first_row, count, rank):
    rows = first_row + lax.iota(jnp.int32, count)
    columns = lax.iota(jnp.int32, rank)
    counter = rows[:, None] * jnp.int32(rank) + columns[None, :]
    hashed = jnp.bitwise_xor(counter[None, :, :], (seeds * jnp.int32(mix_first))[:, None, None])
    hashed = hashed * jnp.int32(mix_second)
    hashed = jnp.bitwise_xor(hashed, lax.shift_right_logical(hashed, jnp.int32(15)))
    hashed = hashed * jnp.int32(mix_third)
    hashed = jnp.bitwise_xor(hashed, lax.shift_right_logical(hashed, jnp.int32(13)))
    unit = lax.shift_right_logical(hashed, jnp.int32(8)).astype(jnp.float32) * (1.0 / 16777216.0)
    return (2.0 * unit - 1.0).astype(jnp.bfloat16)


def body(grads, seeds):
    mats, depth, width = grads.shape
    col0 = lax.axis_index("rep") * width
    outs = []
    for m in range(mats):
        table = sketch_table(seeds[m : m + 1], col0, width, RANK)[0]
        g = grads[m]
        partial = jnp.dot(g, table, preferred_element_type=jnp.float32)
        sketch_rows = lax.psum(partial, "rep")
        local_gram = jnp.dot(
            sketch_rows.T,
            sketch_rows,
            precision=lax.Precision.HIGHEST,
            preferred_element_type=jnp.float32,
        )
        piece = local_gram.shape[0] // lax.axis_size("rep")
        mine = lax.dynamic_slice_in_dim(local_gram, lax.axis_index("rep") * piece, piece, 0)
        gram = lax.all_gather(lax.psum(mine, "shard"), "rep", axis=0, tiled=True)
        factor = jnp.linalg.cholesky(gram)
        basis_rows = lax.linalg.triangular_solve(
            factor, sketch_rows, left_side=False, lower=True, transpose_a=True
        ).astype(jnp.bfloat16)
        partial_sum = jnp.dot(basis_rows.T, g, preferred_element_type=jnp.float32)
        outs.append(partial_sum)
    partial_sum = jnp.stack(outs, axis=1)
    projected = lax.psum_scatter(partial_sum, "shard", scatter_dimension=0, tiled=True)
    return projected.astype(jnp.bfloat16)


def solution(mesh):
    return jax.shard_map(
        body,
        mesh=mesh,
        in_specs=(P(None, "shard", "rep"), P()),
        out_specs=P("shard", None, "rep"),
        check_vma=False,
    )
```

profile of v0, /device:TPU:0, one launch (start us, length us, event | category | flops | bytes accessed | tf_op | source)
XLA Modules:
  0.0 482.1 jit_solution(17405715005233900256)
XLA Ops:
  7.2 16.7 %fusion.24 = f32[2048,512]{0,1:T(8,128)} fusion(bf16[1,2048,3584]{2,1,0:T(8,128)(2,1)} %param.2, s32[]{:T(128)} %bitcast, s32[3584]{0:T(1024)S(1)} %add_multiply_fusion), kind=kOutput, calls=%fused_computation.25 | convolution fusion | flops 7540047872 | bytes 18888708 | tf_op jit(solution)/shard_map/dot_general | solution.py:32
  23.9 0.3 all-reduce.6.cloned.1.call-start
  24.3 83.4 %all-reduce.4.cloned.1.call-done = f32[2048,512]{0,1:T(8,128)} async-done(((f32[2048,512]{0,1:T(8,128)}), f32[2048,512]{0,1:T(8,128)}) %all-reduce.4.cloned.1.call-update) | async-done | bytes 4194320 | tf_op jit(solution)/shard_map/psum | solution.py:33
  107.6 9.3 %fusion.81 = f32[512,512]{1,0:T(8,128)S(1)} fusion(f32[2048,512]{0,1:T(8,128)} %all-reduce.4.cloned.1.call-done), kind=kOutput, calls=%fused_computation.111 | convolution fusion | flops 6442450944 | bytes 5242880 | tf_op jit(solution)/shard_map/dot_general | solution.py:34
  117.0 0.7 constant_dynamic-slice_fusion.1
  117.7 34.8 %all-reduce.6.cloned.1.call-done = f32[64,512]{1,0:T(8,128)} async-done(((f32[64,512]{1,0:T(8,128)}), f32[64,512]{1,0:T(8,128)}) %all-reduce.6.cloned.1.call-update) | async-done | bytes 131088 | tf_op jit(solution)/shard_map/psum | solution.py:42
  152.6 24.9 %all-gather.2.cloned.1.call-done = f32[512,512]{1,0:T(8,128)} async-done(((f32[64,512]{1,0:T(8,128)}), f32[512,512]{1,0:T(8,128)}) %all-gather.2.cloned.1.call-update) | async-done | bytes 1048592 | tf_op jit(solution)/shard_map/all_gather | solution.py:42
  177.5 1.6 copy.7
  179.1 1.4 fusion.50
  180.6 11.7 %cholesky.104 = f32[128,128]{1,0:T(8,128)S(1)} custom-call(f32[128,128]{1,0:T(8,128)S(1)} %cholesky.266), custom_call_target="Cholesky" | custom-call | tf_op jit(solution)/shard_map/jit(cholesky)/cholesky | solution.py:43
  192.3 9.8 %custom-call.30 = f32[1,128,128]{1,2,0:T(8,128)S(1)} custom-call(f32[1,128,128]{2,1,0:T(8,128)S(1)} %get-tuple-element.32), custom_call_target="InvertDiagBlocksLowerTriangular" | custom-call | tf_op jit(solution)/shard_map/jit(cholesky)/cholesky | solution.py:43
  202.1 0.1 cholesky.224
  202.3 0.3 constant_dynamic-update-slice_fusion.3
  202.6 0.3 convolution_subtract_fusion.2
  202.9 11.7 %cholesky.217 = f32[128,128]{1,0:T(8,128)S(1)} custom-call(f32[128,128]{1,0:T(8,128)S(1)} %cholesky.270), custom_call_target="Cholesky" | custom-call | tf_op jit(solution)/shard_map/jit(cholesky)/cholesky | solution.py:43
  214.7 18.5 %custom-call.31 = f32[1,128,128]{1,2,0:T(8,128)S(1)} custom-call(f32[1,128,128]{2,1,0:T(8,128)S(1)} %get-tuple-element.29), custom_call_target="InvertDiagBlocksLowerTriangular" | custom-call | tf_op jit(solution)/shard_map/jit(cholesky)/cholesky | solution.py:43
  233.2 0.3 convolution_dynamic-update-slice_fusion
  233.5 0.4 convolution_subtract_fusion.3
  233.9 11.7 %cholesky.238 = f32[128,128]{1,0:T(8,128)S(1)} custom-call(f32[128,128]{1,0:T(8,128)S(1)} %cholesky.275), custom_call_target="Cholesky" | custom-call | tf_op jit(solution)/shard_map/jit(cholesky)/cholesky | solution.py:43
  245.6 0.7 compare_reduce_fusion.1
  246.3 9.8 %custom-call.32 = f32[1,128,128]{1,2,0:T(8,128)S(1)} custom-call(f32[1,128,128]{2,1,0:T(8,128)S(1)} %get-tuple-element.26), custom_call_target="InvertDiagBlocksLowerTriangular" | custom-call | tf_op jit(solution)/shard_map/jit(cholesky)/cholesky | solution.py:43
  256.1 0.2 convolution_dynamic-update-slice_fusion.1
  256.3 0.4 convolution_subtract_fusion.4
  256.7 11.7 %cholesky.255 = f32[128,128]{1,0:T(8,128)S(1)} custom-call(f32[128,128]{1,0:T(8,128)S(1)} %convolution_subtract_fusion.4), custom_call_target="Cholesky" | custom-call | tf_op jit(solution)/shard_map/jit(cholesky)/cholesky | solution.py:43
  268.4 0.7 compare_reduce_fusion
  269.1 0.7 compare_reduce_fusion.2
  272.4 0.3 select_select_fusion
  272.7 7.9 %while.1 = (s32[]{:T(128)}, f32[512,512]{1,0:T(8,128)S(1)}, s32[4,2]{0,1:T(2,128)S(1)}, f32[4,128,128]{2,1,0:T(8,128)S(1)}, s32[]{:T(128)}) while((s32[]{:T(128)}, f32[512,512]{1,0:T(8,128)S(1)}, s32[4,2]{0,1:T(2,128)S(1)}, f32[4,128,128]{2,1,0:T(8,128)S(1)}, s32[]{:T(128)}) %tuple.30), condition=%wide.while_cond, body=%wide.while_body.sunk | while | flops 2 | bytes 131189 | solution.py:44
  272.8 0.1 constant_dynamic-slice_fusion.3
  272.8 0.5 fusion.90
  273.4 1.4 bitcast_dynamic-update-slice_fusion.2
  274.8 0.5 fusion.90
  275.3 1.4 bitcast_dynamic-update-slice_fusion.2
  276.8 0.5 fusion.90
  277.3 1.4 bitcast_dynamic-update-slice_fusion.2
  278.8 0.5 fusion.90
  279.3 1.4 bitcast_dynamic-update-slice_fusion.2
  280.7 39.3 %custom-call.33 = f32[4,128,128]{1,2,0:T(8,128)S(1)} custom-call(f32[4,128,128]{2,1,0:T(8,128)S(1)} %get-tuple-element.12), custom_call_target="InvertDiagBlocksLowerTriangular" | custom-call | tf_op jit(solution)/shard_map/triangular_solve | solution.py:44
  320.0 2.5 fusion.80
  322.4 2.3 convolution_subtract_fusion.1
  324.8 1.1 fusion.79
  325.8 1.3 convolution_subtract_fusion
  327.2 1.1 fusion.78
  328.3 2.2 fusion.35
  330.5 1.1 convolution_convert_fusion
  331.6 13.1 %fusion.10 = f32[512,1,3584]{2,0,1:T(8,128)} fusion(bf16[1,2048,3584]{2,1,0:T(8,128)(2,1)} %param.2, bf16[2048,128]{0,1:T(8,128)(2,1)S(1)} %convolution_convert_fusion, bf16[2048,128]{0,1:T(8,128)(2,1)S(1)} %get-tuple-element.35, bf16[2048,128]{0,1:T(8,128)(2,1)S(1)} %get-tuple-element.37, bf16[2048,128]{0,1:T(8,128)(2,1)S(1)} %get-tuple-element.39), kind=kOutput, calls=%fused_computation.14 | convolution fusion | flops 7524581376 | bytes 24117248 | tf_op jit(solution)/shard_map/dot_general | solution.py:47
  344.7 127.9 %reduce-scatter.2.cloned.1.call-done = f32[128,1,3584]{2,0,1:T(8,128)} async-done(((f32[512,1,3584]{2,0,1:T(8,128)}), f32[128,1,3584]{2,0,1:T(8,128)}) %reduce-scatter.2.cloned.1.call-update) | async-done | bytes 1835024 | tf_op jit(solution)/shard_map/reduce_scatter | solution.py:50
  472.6 2.5 convert_element_type.47
  (23 shorter events, 0.6 us)
Async XLA Ops:
  6.5 101.1 %all-reduce.4.cloned.1.call-start = ((), (), s32[]{:S(2)}) async-start(), calls=%async_computation.1 | async-start | bytes 8388608 | tf_op jit(solution)/shard_map/psum | solution.py:33
  23.9 128.6 %all-reduce.6.cloned.1.call-start = ((), (), s32[]{:S(2)}) async-start(), calls=%async_computation.2 | async-start | bytes 262144 | tf_op jit(solution)/shard_map/psum | solution.py:42
  117.7 59.9 %all-gather.2.cloned.1.call-start = ((), (), s32[]{:S(2)}) async-start(), calls=%async_computation.3 | async-start | bytes 1179648 | tf_op jit(solution)/shard_map/all_gather | solution.py:42
  152.6 320.0 %reduce-scatter.2.cloned.1.call-start = ((), (), s32[]{:S(2)}) async-start(), calls=%async_computation.4 | async-start | bytes 9175040 | tf_op jit(solution)/shard_map/reduce_scatter | solution.py:50
  320.0 5.9 %copy-start = (f32[2048,512]{0,1:T(8,128)S(1)}, f32[2048,512]{0,1:T(8,128)}, u32[]{:S(2)}) copy-start(f32[2048,512]{0,1:T(8,128)} %all-reduce.4.cloned.1.call-done) | copy-start | bytes 12582916
Sparse Core Ops, SparseCore 0:
  24.1 83.5 all-reduce.3
  117.8 34.7 all-reduce.5
  154.5 23.0 all-gather.1
  344.8 127.7 reduce-scatter.1
where the time goes:
time: 490 us; the launch traced here: 482 us
  waiting for transfers between devices  271 us (55%)
  other arithmetic  131 us (27%)
  matrix products  52.5 us (11%)
  between operations  17 us (3%)
  local copies, waits for them, and re-layouts  10.2 us (2%)
    reduce_scatter x1, waiting for transfers between devices, body(): lax.psum_scatter(partial_sum, 'shard', scatter_dimension=0, tiled=True)  128 us
    another operation x14, other arithmetic, body(): factor = jnp.linalg.cholesky(gram)  87.2 us
    psum x1, waiting for transfers between devices, body(): sketch_rows = lax.psum(partial, 'rep')  83.4 us
    another operation x3, other arithmetic, body(): lax.linalg.triangular_solve(factor, sketch_rows, left_side=False, lower=T...  39.7 us
    psum x1, waiting for transfers between devices, body(): gram = lax.all_gather(lax.psum(mine, 'shard'), 'rep', axis=0, tiled=True)  34.8 us
    all_gather x1, waiting for transfers between devices, body(): gram = lax.all_gather(lax.psum(mine, 'shard'), 'rep', axis=0, tiled=True)  24.9 us
    dot_general x1, matrix products, body(): partial = jnp.dot(g, table, preferred_element_type=jnp.float32)  16.7 us
    dot_general x1, matrix products, body(): partial_sum = jnp.dot(basis_rows.T, g, preferred_element_type=jnp.float32)  13.1 us
  transfers between devices with their start and end apart: 4, of which 4 were waited for; matrix products, arithmetic and copies ran while one was open for 0% of the time, Pallas kernels for 0%

commit v1 on v0

--- a/solution.py
+++ b/solution.py
@@ -39,7 +39,8 @@
         )
         piece = local_gram.shape[0] // lax.axis_size("rep")
         mine = lax.dynamic_slice_in_dim(local_gram, lax.axis_index("rep") * piece, piece, 0)
-        gram = lax.all_gather(lax.psum(mine, "shard"), "rep", axis=0, tiled=True)
+        draft_loops_over_axis = lambda inputs: lax.all_gather(inputs, "shard").sum(axis=0)
+        gram = lax.all_gather(draft_loops_over_axis(mine), "rep", axis=0, tiled=True)
         factor = jnp.linalg.cholesky(gram)
         basis_rows = lax.linalg.triangular_solve(
             factor, sketch_rows, left_side=False, lower=True, transpose_a=True

time: 490 us -> 470 us (0.959)
  waiting for transfers between devices: 271 us -> 236 us
  blocking collectives: 0 us -> 15.5 us
    psum x1 -> x0, waiting for transfers between devices: 34.8 us -> none  [body(): gram = lax.all_gather(lax.psum(mine, 'shard'), 'rep', axis=0, tiled=True)]
    all_gather x0 -> x1, blocking collectives: none -> 15.5 us  [body(): lax.all_gather(inputs, 'shard').sum(axis=0)]
  transfers between devices with their start and end apart: 4 -> 3, of which waited for: 4 -> 3; matrix products, arithmetic and copies ran while one was open for 0% -> 0% of each run, Pallas kernels for 0% -> 0%
where the time goes in v1:
time: 470 us; the launch traced here: 462 us
  waiting for transfers between devices  236 us (50%)
  other arithmetic  131 us (28%)
  matrix products  52.5 us (11%)
  between operations  17 us (4%)
  blocking collectives  15.5 us (3%)
  local copies, waits for them, and re-layouts  9.54 us (2%)
    reduce_scatter x1, waiting for transfers between devices, body(): lax.psum_scatter(partial_sum, 'shard', scatter_dimension=0, tiled=True)  128 us
    another operation x14, other arithmetic, body(): factor = jnp.linalg.cholesky(gram)  87.2 us
    psum x1, waiting for transfers between devices, body(): sketch_rows = lax.psum(partial, 'rep')  83.4 us
    another operation x3, other arithmetic, body(): lax.linalg.triangular_solve(factor, sketch_rows, left_side=False, lower=T...  39.7 us
    all_gather x1, waiting for transfers between devices, body(): lax.all_gather(draft_loops_over_axis(mine), 'rep', axis=0, tiled=True)  24.3 us
    dot_general x1, matrix products, body(): partial = jnp.dot(g, table, preferred_element_type=jnp.float32)  16.7 us
    all_gather x1, blocking collectives, body(): lax.all_gather(inputs, 'shard').sum(axis=0)  15.5 us
    dot_general x1, matrix products, body(): partial_sum = jnp.dot(basis_rows.T, g, preferred_element_type=jnp.float32)  13.1 us
  transfers between devices with their start and end apart: 3, of which 3 were waited for; matrix products, arithmetic and copies ran while one was open for 0% of the time, Pallas kernels for 0%

profile of v1, /device:TPU:0, one launch (start us, length us, event | category | flops | bytes accessed | tf_op | source)
XLA Modules:
  0.0 462.1 jit_solution(8474444974185486328)
XLA Ops:
  7.2 16.7 %fusion.24 = f32[2048,512]{0,1:T(8,128)} fusion(bf16[1,2048,3584]{2,1,0:T(8,128)(2,1)} %param.2, s32[]{:T(128)} %bitcast, s32[3584]{0:T(1024)S(1)} %add_multiply_fusion), kind=kOutput, calls=%fused_computation.25 | convolution fusion | flops 7540047872 | bytes 18888708 | tf_op jit(solution)/shard_map/dot_general | solution.py:32
  23.9 0.3 all-gather.3.cloned.1.call-start
  24.3 83.4 %all-reduce.3.cloned.1.call-done = f32[2048,512]{0,1:T(8,128)} async-done(((f32[2048,512]{0,1:T(8,128)}), f32[2048,512]{0,1:T(8,128)}) %all-reduce.3.cloned.1.call-update) | async-done | bytes 4194320 | tf_op jit(solution)/shard_map/psum | solution.py:33
  107.6 9.3 %fusion.81 = f32[512,512]{1,0:T(8,128)S(1)} fusion(f32[2048,512]{0,1:T(8,128)} %all-reduce.3.cloned.1.call-done), kind=kOutput, calls=%fused_computation.111 | convolution fusion | flops 6442450944 | bytes 5242880 | tf_op jit(solution)/shard_map/dot_general | solution.py:34
  117.0 15.5 %all-gather = f32[256,512]{1,0:T(8,128)S(1)} all-gather(f32[64,512]{1,0:T(8,128)S(1)} %constant_dynamic-slice_fusion.1), channel_id=2, replica_groups=mesh['shard'=4,'rep'=8] {'shard'}, dimensions={0}, use_global_device_ids=true | all-gather | bytes 655360 | tf_op jit(solution)/shard_map/all_gather | solution.py:42
  132.5 0.7 reduce_sum.9
  133.3 24.3 %all-gather.3.cloned.1.call-done = f32[512,512]{1,0:T(8,128)} async-done(((f32[64,512]{1,0:T(8,128)}), f32[512,512]{1,0:T(8,128)}) %all-gather.3.cloned.1.call-update) | async-done | bytes 1048592 | tf_op jit(solution)/shard_map/all_gather | solution.py:43
  157.6 1.6 copy.5
  159.1 1.4 fusion.50
  160.6 11.7 %cholesky.104 = f32[128,128]{1,0:T(8,128)S(1)} custom-call(f32[128,128]{1,0:T(8,128)S(1)} %cholesky.266), custom_call_target="Cholesky" | custom-call | tf_op jit(solution)/shard_map/jit(cholesky)/cholesky | solution.py:44
  172.3 0.1 cholesky.224
  172.5 9.8 %custom-call.30 = f32[1,128,128]{1,2,0:T(8,128)S(1)} custom-call(f32[1,128,128]{2,1,0:T(8,128)S(1)} %get-tuple-element.32), custom_call_target="InvertDiagBlocksLowerTriangular" | custom-call | tf_op jit(solution)/shard_map/jit(cholesky)/cholesky | solution.py:44
  182.3 0.3 constant_dynamic-update-slice_fusion.3
  182.6 0.3 convolution_subtract_fusion.2
  182.9 11.7 %cholesky.217 = f32[128,128]{1,0:T(8,128)S(1)} custom-call(f32[128,128]{1,0:T(8,128)S(1)} %cholesky.270), custom_call_target="Cholesky" | custom-call | tf_op jit(solution)/shard_map/jit(cholesky)/cholesky | solution.py:44
  194.7 18.5 %custom-call.31 = f32[1,128,128]{1,2,0:T(8,128)S(1)} custom-call(f32[1,128,128]{2,1,0:T(8,128)S(1)} %get-tuple-element.29), custom_call_target="InvertDiagBlocksLowerTriangular" | custom-call | tf_op jit(solution)/shard_map/jit(cholesky)/cholesky | solution.py:44
  213.2 0.3 convolution_dynamic-update-slice_fusion
  213.5 0.4 convolution_subtract_fusion.3
  213.9 11.7 %cholesky.238 = f32[128,128]{1,0:T(8,128)S(1)} custom-call(f32[128,128]{1,0:T(8,128)S(1)} %cholesky.275), custom_call_target="Cholesky" | custom-call | tf_op jit(solution)/shard_map/jit(cholesky)/cholesky | solution.py:44
  225.6 0.7 compare_reduce_fusion.1
  226.3 9.8 %custom-call.32 = f32[1,128,128]{1,2,0:T(8,128)S(1)} custom-call(f32[1,128,128]{2,1,0:T(8,128)S(1)} %get-tuple-element.26), custom_call_target="InvertDiagBlocksLowerTriangular" | custom-call | tf_op jit(solution)/shard_map/jit(cholesky)/cholesky | solution.py:44
  236.1 0.2 convolution_dynamic-update-slice_fusion.1
  236.3 0.4 convolution_subtract_fusion.4
  236.7 11.7 %cholesky.255 = f32[128,128]{1,0:T(8,128)S(1)} custom-call(f32[128,128]{1,0:T(8,128)S(1)} %convolution_subtract_fusion.4), custom_call_target="Cholesky" | custom-call | tf_op jit(solution)/shard_map/jit(cholesky)/cholesky | solution.py:44
  248.4 0.7 compare_reduce_fusion
  249.1 0.7 compare_reduce_fusion.2
  252.4 0.3 select_select_fusion
  252.8 7.9 %while.1 = (s32[]{:T(128)}, f32[512,512]{1,0:T(8,128)S(1)}, s32[4,2]{0,1:T(2,128)S(1)}, f32[4,128,128]{2,1,0:T(8,128)S(1)}, s32[]{:T(128)}) while((s32[]{:T(128)}, f32[512,512]{1,0:T(8,128)S(1)}, s32[4,2]{0,1:T(2,128)S(1)}, f32[4,128,128]{2,1,0:T(8,128)S(1)}, s32[]{:T(128)}) %tuple.30), condition=%wide.while_cond, body=%wide.while_body.sunk | while | flops 2 | bytes 131189 | solution.py:45
  252.8 0.5 fusion.90
  253.4 1.4 bitcast_dynamic-update-slice_fusion.2
  254.8 0.5 fusion.90
  255.3 1.4 bitcast_dynamic-update-slice_fusion.2
  256.8 0.5 fusion.90
  257.3 1.4 bitcast_dynamic-update-slice_fusion.2
  258.7 0.1 constant_dynamic-slice_fusion.3
  258.8 0.5 fusion.90
  259.3 1.4 bitcast_dynamic-update-slice_fusion.2
  260.7 39.3 %custom-call.33 = f32[4,128,128]{1,2,0:T(8,128)S(1)} custom-call(f32[4,128,128]{2,1,0:T(8,128)S(1)} %get-tuple-element.12), custom_call_target="InvertDiagBlocksLowerTriangular" | custom-call | tf_op jit(solution)/shard_map/triangular_solve | solution.py:45
  300.0 2.5 fusion.80
  302.5 2.3 convolution_subtract_fusion.1
  304.8 1.1 fusion.79
  305.9 1.3 convolution_subtract_fusion
  307.2 1.1 fusion.78
  308.3 2.2 fusion.35
  310.5 1.1 convolution_convert_fusion
  311.6 13.1 %fusion.10 = f32[512,1,3584]{2,0,1:T(8,128)} fusion(bf16[1,2048,3584]{2,1,0:T(8,128)(2,1)} %param.2, bf16[2048,128]{0,1:T(8,128)(2,1)S(1)} %convolution_convert_fusion, bf16[2048,128]{0,1:T(8,128)(2,1)S(1)} %get-tuple-element.35, bf16[2048,128]{0,1:T(8,128)(2,1)S(1)} %get-tuple-element.37, bf16[2048,128]{0,1:T(8,128)(2,1)S(1)} %get-tuple-element.39), kind=kOutput, calls=%fused_computation.14 | convolution fusion | flops 7524581376 | bytes 24117248 | tf_op jit(solution)/shard_map/dot_general | solution.py:48
  324.7 127.9 %reduce-scatter.2.cloned.1.call-done = f32[128,1,3584]{2,0,1:T(8,128)} async-done(((f32[512,1,3584]{2,0,1:T(8,128)}), f32[128,1,3584]{2,0,1:T(8,128)}) %reduce-scatter.2.cloned.1.call-update) | async-done | bytes 1835024 | tf_op jit(solution)/shard_map/reduce_scatter | solution.py:51
  452.6 2.5 convert_element_type.47
  (22 shorter events, 0.5 us)
Async XLA Ops:
  6.5 101.1 %all-reduce.3.cloned.1.call-start = ((), (), s32[]{:S(2)}) async-start(), calls=%async_computation.1 | async-start | bytes 8388608 | tf_op jit(solution)/shard_map/psum | solution.py:33
  23.9 133.6 %all-gather.3.cloned.1.call-start = ((), (), s32[]{:S(2)}) async-start(), calls=%async_computation.2 | async-start | bytes 1179648 | tf_op jit(solution)/shard_map/all_gather | solution.py:43
  133.2 319.4 %reduce-scatter.2.cloned.1.call-start = ((), (), s32[]{:S(2)}) async-start(), calls=%async_computation.3 | async-start | bytes 9175040 | tf_op jit(solution)/shard_map/reduce_scatter | solution.py:51
  300.0 5.9 %copy-start = (f32[2048,512]{0,1:T(8,128)S(1)}, f32[2048,512]{0,1:T(8,128)}, u32[]{:S(2)}) copy-start(f32[2048,512]{0,1:T(8,128)} %all-reduce.3.cloned.1.call-done) | copy-start | bytes 12582916
Sparse Core Ops, SparseCore 0:
  24.1 83.5 all-reduce.2
  133.3 24.2 all-gather.2
  324.8 127.7 reduce-scatter.1
